TPU v7x, 32 devices: a whole 2x2x4 slice. The times are simulated.
32 devices in a mesh: ctx: 8 (over z, y), fsdp: 4 (over x, core).
Axes of the slice: x: 2, y: 2, z: 4, core: 2. Of those that a mesh axis runs over, the one named last changes fastest.
Arguments:
- tokens: bfloat16 [24, 1024, 896], P('fsdp', 'ctx'), may hold values from -6 to 6
- norm_one: bfloat16 [896], P('fsdp'), may hold values from 0.5 to 1.5
- query_weight: bfloat16 [896, 896], P('fsdp'), may hold values from -0.1875 to 0.1875
- query_bias: bfloat16 [896], P('fsdp'), may hold values from -3 to 3
- key_weight: bfloat16 [896, 128], P('fsdp'), may hold values from -0.1875 to 0.1875
- key_bias: bfloat16 [128], P('fsdp'), may hold values from -3 to 3
- value_weight: bfloat16 [896, 128], P('fsdp'), may hold values from -0.1875 to 0.1875
- value_bias: bfloat16 [128], P('fsdp'), may hold values from -3 to 3
- output_weight: bfloat16 [896, 896], P('fsdp'), may hold values from -0.75 to 0.75
- norm_two: bfloat16 [896], P('fsdp'), may hold values from 0.5 to 1.5
- gate_up: bfloat16 [2, 896, 4864], P(None, None, 'fsdp'), may hold values from -0.1875 to 0.1875
- down_weight: bfloat16 [4864, 896], P('fsdp'), may hold values from -0.078125 to 0.078125
- cotangent: bfloat16 [24, 1024, 896], P('fsdp', 'ctx'), may hold values from -6 to 6
Outputs:
- layer_out: bfloat16 [24, 1024, 896], P('fsdp', 'ctx')
- token_grad: float32 [24, 1024, 896], P('fsdp', 'ctx')
- norm_one_grad: float32 [896], P('fsdp')
- query_weight_grad: float32 [896, 896], P('fsdp')
- query_bias_grad: float32 [896], P('fsdp')
- key_weight_grad: float32 [896, 128], P('fsdp')
- key_bias_grad: float32 [128], P('fsdp')
- value_weight_grad: float32 [896, 128], P('fsdp')
- value_bias_grad: float32 [128], P('fsdp')
- output_weight_grad: float32 [896, 896], P('fsdp')
- norm_two_grad: float32 [896], P('fsdp')
- gate_up_grad: float32 [2, 896, 4864], P(None, None, 'fsdp')
- down_weight_grad: float32 [4864, 896], P('fsdp')
All inputs are finite; a program needn't handle non-finite values.
Results may differ from a plain program's by a relative error of at most 0.03.
Values may be sent and summed in bfloat16 or wider, within the bound.
No kernel may reach another device: no remote copies, remote signals or barrier semaphores. Data moves between devices by JAX's collectives and lax.ppermute only.
A program may use at most 320 MiB of HBM per device.

v0:
```python
import math

import jax
import jax.numpy as jnp
from jax import lax
from jax.sharding import PartitionSpec as P

HEADS = 14
KV_HEADS = 2
HEAD_DIM = 64


NORM_EPSILON = 1e-06
ROPE_BASE = 1000000.0
MASKED_SCORE = -1e30


def rotary(positions):
    half_dim = HEAD_DIM // 2
    exponent = jnp.arange(half_dim, dtype=jnp.float32) * (2.0 / HEAD_DIM)
    frequency = ROPE_BASE ** (-exponent)
    angles = positions.astype(jnp.float32)[:, None] * frequency[None, :]
    angles = jnp.concatenate([angles, angles], axis=1)
    return (jnp.cos(angles), jnp.sin(angles))


def rotate(moving, cosine, sine_table):
    half_dim = moving.shape[-1] // 2
    turned = jnp.concatenate([-moving[..., half_dim:], moving[..., :half_dim]], axis=-1)
    return moving * cosine[:, None, :] + turned * sine_table[:, None, :]


def rms_norm(moving, gain):
    return (
        moving * lax.rsqrt(jnp.mean(moving * moving, axis=-1, keepdims=True) + NORM_EPSILON) * gain
    )


def swish(gate_part, up_part):
    return jax.nn.silu(gate_part) * up_part


def mix_in(carried, key_rows, value_rows, query_heads, query_pos):
    seq_count, row_count, _ = key_rows.shape
    step_rows = math.gcd(row_count, 512)
    step_count = row_count // step_rows
    scale = HEAD_DIM ** (-0.5)

    def one_step(current, step_index):
        begin = step_index * step_rows

        def one_compute(present):
            row_top, row_total, summed = present
            key_part = lax.dynamic_slice_in_dim(
                key_rows, step_index * step_rows, step_rows, 1
            ).reshape(seq_count, step_rows, KV_HEADS, HEAD_DIM)
            value_part = lax.dynamic_slice_in_dim(
                value_rows, step_index * step_rows, step_rows, 1
            ).reshape(seq_count, step_rows, KV_HEADS, HEAD_DIM)
            scores = (
                jnp.einsum(
                    "sgjtd,srgd->sgjtr", query_heads, key_part, preferred_element_type=jnp.float32
                )
                * scale
            )
            allowed = (begin + jnp.arange(step_rows, dtype=jnp.int32))[None, :] <= query_pos[
                :, None
            ]
            masked = jnp.where(allowed, scores, MASKED_SCORE)
            new_top = jnp.maximum(row_top, jnp.max(masked, axis=-1))
            weights = jnp.where(allowed, jnp.exp(masked - new_top[..., None]), 0.0)
            rescale = jnp.exp(row_top - new_top)
            new_total = row_total * rescale + jnp.sum(weights, axis=-1)
            new_sum = summed * rescale[..., None] + jnp.einsum(
                "sgjtr,srgd->sgjtd",
                weights.astype(jnp.bfloat16),
                value_part,
                preferred_element_type=jnp.float32,
            )
            return (new_top, new_total, new_sum)

        return (
            lax.cond(begin <= query_pos[-1], one_compute, lambda kept_state: kept_state, current),
            None,
        )

    carried, _ = lax.scan(one_step, carried, jnp.arange(step_count, dtype=jnp.int32))
    return carried


def shards(
    tokens,
    norm_one,
    query_weight,
    query_bias,
    key_weight,
    key_bias,
    value_weight,
    value_bias,
    output_weight,
    norm_two,
    gate_up,
    down_weight,
    cotangent,
):
    seq_count, block_rows, model_width = tokens.shape
    group_size = HEADS // KV_HEADS
    kv_width = KV_HEADS * HEAD_DIM
    q_width = HEADS * HEAD_DIM
    scale = HEAD_DIM ** (-0.5)
    full_length = lax.axis_size("ctx") * block_rows
    query_pos = lax.axis_index("ctx") * block_rows + jnp.arange(block_rows, dtype=jnp.int32)
    cosine, sine_table = rotary(query_pos)
    (
        gain_one,
        query_full,
        qbias_full,
        key_full,
        kbias_full,
        value_full,
        vbias_full,
        output_full,
        gain_two,
    ) = (
        lax.all_gather(norm_one, "fsdp", axis=0, tiled=True),
        lax.all_gather(query_weight, "fsdp", axis=0, tiled=True),
        lax.all_gather(query_bias, "fsdp", axis=0, tiled=True),
        lax.all_gather(key_weight, "fsdp", axis=0, tiled=True),
        lax.all_gather(key_bias, "fsdp", axis=0, tiled=True),
        lax.all_gather(value_weight, "fsdp", axis=0, tiled=True),
        lax.all_gather(value_bias, "fsdp", axis=0, tiled=True),
        lax.all_gather(output_weight, "fsdp", axis=0, tiled=True),
        lax.all_gather(norm_two, "fsdp", axis=0, tiled=True),
    )
    tokens_f = tokens.astype(jnp.float32)
    normed, norm_pull = jax.vjp(rms_norm, tokens_f, gain_one.astype(jnp.float32))
    normed_low = normed.astype(jnp.bfloat16)
    query_pre = jnp.einsum(
        "std,de->ste", normed_low, query_full, preferred_element_type=jnp.float32
    ) + qbias_full.astype(jnp.float32)
    key_pre = jnp.einsum(
        "std,de->ste", normed_low, key_full, preferred_element_type=jnp.float32
    ) + kbias_full.astype(jnp.float32)
    value_pre = jnp.einsum(
        "std,de->ste", normed_low, value_full, preferred_element_type=jnp.float32
    ) + vbias_full.astype(jnp.float32)
    value_low = value_pre.astype(jnp.bfloat16)

    def turn(moving):
        return rotate(moving, cosine, sine_table)

    query_rot, query_turn_back = jax.vjp(
        turn, query_pre.reshape(seq_count, block_rows, HEADS, HEAD_DIM)
    )
    key_rot, key_turn_back = jax.vjp(
        turn, key_pre.reshape(seq_count, block_rows, KV_HEADS, HEAD_DIM)
    )
    query_heads = (
        query_rot.astype(jnp.bfloat16)
        .reshape(seq_count, block_rows, KV_HEADS, group_size, HEAD_DIM)
        .transpose(0, 2, 3, 1, 4)
    )
    key_low = key_rot.astype(jnp.bfloat16).reshape(seq_count, block_rows, kv_width)
    stat_shape = (seq_count, KV_HEADS, group_size, block_rows)
    init_state = (
        jnp.full(stat_shape, MASKED_SCORE, jnp.float32),
        jnp.zeros(stat_shape, jnp.float32),
        jnp.zeros(stat_shape + (HEAD_DIM,), jnp.float32),
    )
    row_top, row_total, summed = mix_in(
        init_state,
        lax.all_gather(key_low, "ctx", axis=1, tiled=True),
        lax.all_gather(value_low, "ctx", axis=1, tiled=True),
        query_heads,
        query_pos,
    )
    attention = summed / row_total[..., None]
    log_total = row_top + jnp.log(row_total)
    mixed_low = (
        attention.transpose(0, 3, 1, 2, 4)
        .reshape(seq_count, block_rows, q_width)
        .astype(jnp.bfloat16)
    )
    branch = jnp.einsum("ste,ed->std", mixed_low, output_full, preferred_element_type=jnp.float32)
    hidden = tokens_f + branch
    normed_two, norm_two_pull = jax.vjp(rms_norm, hidden, gain_two.astype(jnp.float32))
    normed_two_low = normed_two.astype(jnp.bfloat16)
    cot_f = cotangent.astype(jnp.float32)
    gate_up_full, down_full = (
        lax.all_gather(gate_up, "fsdp", axis=2, tiled=True),
        lax.all_gather(down_weight, "fsdp", axis=0, tiled=True),
    )
    gate_part = jnp.einsum(
        "std,df->stf", normed_two_low, gate_up_full[0], preferred_element_type=jnp.float32
    )
    up_part = jnp.einsum(
        "std,df->stf", normed_two_low, gate_up_full[1], preferred_element_type=jnp.float32
    )
    inner_act, swish_pull = jax.vjp(swish, gate_part, up_part)
    inner_low = inner_act.astype(jnp.bfloat16)
    ffn_term = jnp.einsum("stf,fd->std", inner_low, down_full, preferred_element_type=jnp.float32)
    grad_down = jnp.einsum("stf,std->fd", inner_low, cotangent, preferred_element_type=jnp.float32)
    grad_inner = jnp.einsum("std,fd->stf", cotangent, down_full, preferred_element_type=jnp.float32)
    grad_gate, grad_up = swish_pull(grad_inner)
    grad_pair = jnp.stack([grad_gate, grad_up]).astype(jnp.bfloat16)
    grad_gate_up = jnp.einsum(
        "std,cstf->cdf", normed_two_low, grad_pair, preferred_element_type=jnp.float32
    )
    grad_normed_two = jnp.einsum(
        "cstf,cdf->std", grad_pair, gate_up_full, preferred_element_type=jnp.float32
    )
    grad_gate_up, grad_down = (
        lax.psum_scatter(
            grad_gate_up.astype(jnp.bfloat16), "fsdp", scatter_dimension=2, tiled=True
        ).astype(jnp.float32),
        lax.psum_scatter(
            grad_down.astype(jnp.bfloat16), "fsdp", scatter_dimension=0, tiled=True
        ).astype(jnp.float32),
    )
    layer_out = (hidden + ffn_term).astype(jnp.bfloat16)
    grad_hidden_norm, grad_gain_two = norm_two_pull(grad_normed_two)
    grad_hidden = cot_f + grad_hidden_norm
    grad_branch = grad_hidden.astype(jnp.bfloat16)
    grad_output = jnp.einsum(
        "ste,std->ed", mixed_low, grad_branch, preferred_element_type=jnp.float32
    )
    grad_mixed = jnp.einsum(
        "std,ed->ste", grad_branch, output_full, preferred_element_type=jnp.float32
    ).astype(jnp.bfloat16)
    grad_heads = grad_mixed.reshape(
        seq_count, block_rows, KV_HEADS, group_size, HEAD_DIM
    ).transpose(0, 2, 3, 1, 4)
    row_delta = jnp.sum(grad_heads.astype(jnp.float32) * attention, axis=-1)
    back_keys, back_values = (
        lax.all_gather(key_low, "ctx", axis=1, tiled=True),
        lax.all_gather(value_low, "ctx", axis=1, tiled=True),
    )
    step_rows = math.gcd(full_length, 512)

    def back_step(current, step_index):
        begin = step_index * step_rows

        def back_compute(present):
            grad_query, grad_kv = present
            key_part = lax.dynamic_slice_in_dim(back_keys, begin, step_rows, 1).reshape(
                seq_count, step_rows, KV_HEADS, HEAD_DIM
            )
            value_part = lax.dynamic_slice_in_dim(back_values, begin, step_rows, 1).reshape(
                seq_count, step_rows, KV_HEADS, HEAD_DIM
            )
            scores = (
                jnp.einsum(
                    "sgjtd,srgd->sgjtr", query_heads, key_part, preferred_element_type=jnp.float32
                )
                * scale
            )
            allowed = (begin + jnp.arange(step_rows, dtype=jnp.int32))[None, :] <= query_pos[
                :, None
            ]
            probs = jnp.where(allowed, jnp.exp(scores - log_total[..., None]), 0.0)
            grad_probs = jnp.einsum(
                "sgjtd,srgd->sgjtr", grad_heads, value_part, preferred_element_type=jnp.float32
            )
            grad_scores = (scale * probs * (grad_probs - row_delta[..., None])).astype(jnp.bfloat16)
            grad_query = grad_query + jnp.einsum(
                "sgjtr,srgd->sgjtd", grad_scores, key_part, preferred_element_type=jnp.float32
            )
            grad_key = jnp.einsum(
                "sgjtr,sgjtd->srgd", grad_scores, query_heads, preferred_element_type=jnp.float32
            )
            grad_value = jnp.einsum(
                "sgjtr,sgjtd->srgd",
                probs.astype(jnp.bfloat16),
                grad_heads,
                preferred_element_type=jnp.float32,
            )
            joined = jnp.concatenate(
                [
                    grad_key.reshape(seq_count, step_rows, kv_width),
                    grad_value.reshape(seq_count, step_rows, kv_width),
                ],
                axis=2,
            )
            return (grad_query, lax.dynamic_update_slice_in_dim(grad_kv, joined, begin, 1))

        return (
            lax.cond(begin <= query_pos[-1], back_compute, lambda kept_state: kept_state, current),
            None,
        )

    back_init = (
        jnp.zeros(stat_shape + (HEAD_DIM,), jnp.float32),
        jnp.zeros((seq_count, full_length, 2 * kv_width), jnp.float32),
    )
    (grad_query, grad_kv_all), _ = lax.scan(
        back_step, back_init, jnp.arange(full_length // step_rows, dtype=jnp.int32)
    )
    grad_kv = lax.psum_scatter(
        grad_kv_all.astype(jnp.bfloat16), "ctx", scatter_dimension=1, tiled=True
    ).astype(jnp.float32)
    grad_key_rot = grad_kv[..., :kv_width].reshape(seq_count, block_rows, KV_HEADS, HEAD_DIM)
    grad_key_low = (
        key_turn_back(grad_key_rot)[0].reshape(seq_count, block_rows, kv_width).astype(jnp.bfloat16)
    )
    grad_value_low = grad_kv[..., kv_width:].astype(jnp.bfloat16)
    grad_query_rot = grad_query.transpose(0, 3, 1, 2, 4).reshape(
        seq_count, block_rows, HEADS, HEAD_DIM
    )
    grad_query_low = (
        query_turn_back(grad_query_rot)[0]
        .reshape(seq_count, block_rows, q_width)
        .astype(jnp.bfloat16)
    )
    grad_qbias = jnp.sum(grad_query_low.astype(jnp.float32), axis=(0, 1))
    grad_kbias = jnp.sum(grad_key_low.astype(jnp.float32), axis=(0, 1))
    grad_vbias = jnp.sum(grad_value_low.astype(jnp.float32), axis=(0, 1))
    grad_qweight = jnp.einsum(
        "std,ste->de", normed_low, grad_query_low, preferred_element_type=jnp.float32
    )
    grad_kweight = jnp.einsum(
        "std,ste->de", normed_low, grad_key_low, preferred_element_type=jnp.float32
    )
    grad_vweight = jnp.einsum(
        "std,ste->de", normed_low, grad_value_low, preferred_element_type=jnp.float32
    )
    grad_normed = jnp.einsum(
        "ste,de->std", grad_query_low, query_full, preferred_element_type=jnp.float32
    )
    grad_normed = grad_normed + jnp.einsum(
        "ste,de->std", grad_key_low, key_full, preferred_element_type=jnp.float32
    )
    grad_normed = grad_normed + jnp.einsum(
        "ste,de->std", grad_value_low, value_full, preferred_element_type=jnp.float32
    )
    grad_tokens_norm, grad_gain_one = norm_pull(grad_normed)
    token_grad = grad_hidden + grad_tokens_norm
    (
        owned_gain_one,
        owned_qweight,
        owned_qbias,
        owned_kweight,
        owned_kbias,
        owned_vweight,
        owned_vbias,
        owned_output,
        owned_gain_two,
    ) = (
        lax.psum_scatter(
            grad_gain_one.astype(jnp.bfloat16), "fsdp", scatter_dimension=0, tiled=True
        ).astype(jnp.float32),
        lax.psum_scatter(
            grad_qweight.astype(jnp.bfloat16), "fsdp", scatter_dimension=0, tiled=True
        ).astype(jnp.float32),
        lax.psum_scatter(
            grad_qbias.astype(jnp.bfloat16), "fsdp", scatter_dimension=0, tiled=True
        ).astype(jnp.float32),
        lax.psum_scatter(
            grad_kweight.astype(jnp.bfloat16), "fsdp", scatter_dimension=0, tiled=True
        ).astype(jnp.float32),
        lax.psum_scatter(
            grad_kbias.astype(jnp.bfloat16), "fsdp", scatter_dimension=0, tiled=True
        ).astype(jnp.float32),
        lax.psum_scatter(
            grad_vweight.astype(jnp.bfloat16), "fsdp", scatter_dimension=0, tiled=True
        ).astype(jnp.float32),
        lax.psum_scatter(
            grad_vbias.astype(jnp.bfloat16), "fsdp", scatter_dimension=0, tiled=True
        ).astype(jnp.float32),
        lax.psum_scatter(
            grad_output.astype(jnp.bfloat16), "fsdp", scatter_dimension=0, tiled=True
        ).astype(jnp.float32),
        lax.psum_scatter(
            grad_gain_two.astype(jnp.bfloat16), "fsdp", scatter_dimension=0, tiled=True
        ).astype(jnp.float32),
    )
    (
        sum_gain_one,
        sum_qweight,
        sum_qbias,
        sum_kweight,
        sum_kbias,
        sum_vweight,
        sum_vbias,
        sum_output,
        sum_gain_two,
        sum_gate_up,
        sum_down,
    ) = (
        lax.psum(owned_gain_one.astype(jnp.bfloat16), "ctx").astype(jnp.float32),
        lax.psum(owned_qweight.astype(jnp.bfloat16), "ctx").astype(jnp.float32),
        lax.psum(owned_qbias.astype(jnp.bfloat16), "ctx").astype(jnp.float32),
        lax.psum(owned_kweight.astype(jnp.bfloat16), "ctx").astype(jnp.float32),
        lax.psum(owned_kbias.astype(jnp.bfloat16), "ctx").astype(jnp.float32),
        lax.psum(owned_vweight.astype(jnp.bfloat16), "ctx").astype(jnp.float32),
        lax.psum(owned_vbias.astype(jnp.bfloat16), "ctx").astype(jnp.float32),
        lax.psum(owned_output.astype(jnp.bfloat16), "ctx").astype(jnp.float32),
        lax.psum(owned_gain_two.astype(jnp.bfloat16), "ctx").astype(jnp.float32),
        lax.psum(grad_gate_up.astype(jnp.bfloat16), "ctx").astype(jnp.float32),
        lax.psum(grad_down.astype(jnp.bfloat16), "ctx").astype(jnp.float32),
    )
    return (
        layer_out,
        token_grad,
        sum_gain_one,
        sum_qweight,
        sum_qbias,
        sum_kweight,
        sum_kbias,
        sum_vweight,
        sum_vbias,
        sum_output,
        sum_gain_two,
        sum_gate_up,
        sum_down,
    )


def solution(mesh):
    placed = (
        P("fsdp", "ctx", None),
        P("fsdp"),
        P("fsdp", None),
        P("fsdp"),
        P("fsdp", None),
        P("fsdp"),
        P("fsdp", None),
        P("fsdp"),
        P("fsdp", None),
        P("fsdp"),
        P(None, None, "fsdp"),
        P("fsdp", None),
        P("fsdp", "ctx", None),
    )
    return jax.shard_map(
        shards,
        mesh=mesh,
        in_specs=placed,
        out_specs=(
            P("fsdp", "ctx", None),
            P("fsdp", "ctx", None),
            P("fsdp"),
            P("fsdp", None),
            P("fsdp"),
            P("fsdp", None),
            P("fsdp"),
            P("fsdp", None),
            P("fsdp"),
            P("fsdp", None),
            P("fsdp"),
            P(None, None, "fsdp"),
            P("fsdp", None),
        ),
        check_vma=False,
    )
```

profile of v0, /device:TPU:0, one launch (start us, length us, event | category | flops | bytes accessed | tf_op | source)
XLA Modules:
  0.0 1387.1 jit_solution(8661710070409432026)
XLA Ops:
  14.9 8.6 all-reduce.17
  23.5 7.2 all_gather.47
  43.8 20.1 %copy.81 = bf16[2,896,1216]{1,0,2:T(2,128)(2,1)} copy(bf16[2,896,1216]{1,2,0:T(8,128)(2,1)} %param.31) | data formatting | bytes 8716288 | tf_op args[10]
  82.2 43.7 %all-gather.7.cloned.1.call-done = bf16[6,1024,128]{1,2,0:T(8,128)(2,1)} async-done(((bf16[6,128,128]{1,2,0:T(8,128)(2,1)}), bf16[6,1024,128]{1,2,0:T(8,128)(2,1)}) %all-gather.7.cloned.1.call-update) | async-done | bytes 1572880 | tf_op jit(solution)/shard_map/all_gather | solution.py:172
  127.8 30.4 %while.26 = (s32[]{:T(128)}, f32[6,2,7,128]{3,2,1,0:T(8,128)S(1)}, f32[6,2,7,128]{3,2,1,0:T(8,128)S(1)}, f32[6,2,7,128,64]{3,4,2,1,0:T(8,128)}, s32[2]{0:T(128)S...) while((s32[]{:T(128)}, f32[6,2,7,128]{3,2,1,0:T(8,128)S(1)}, ...), condition=%wide.region_6.7_spmd, body=%wide.region_1.6_spmd.sunk | while | flops 1482315264 | bytes 166695824 | solution.py:87
  130.3 25.2 %conditional.4 = ((f32[6,2,7,128]{3,2,1,0:T(8,128)S(1)}, f32[6,2,7,128]{3,2,1,0:T(8,128)S(1)}, f32[6,2,7,128,64]{3,4,2,1,0:T(8,128)})) conditional(s32[]{:T(128)} %convert_element_type.308, (f32[6,2,7,128]{3,2,1,0:T(8,128)S(1)}, f32[6,2,7,128]{3,2,1,0:T(8,128)S(1)}, f32[6,2,7,128,64]{3,4,2,1,0:T(8,128)}) %tuple.81, (s32[]{:T(128)}, s32[128]{0:T(128)S(1)}, ...), branch_computations={%region_2.2_spmd, %region_3.5_spmd} | conditional | flops 1482315264 | bytes 166695552 | solution.py:83
  143.0 12.5 multiply_add_fusion
  168.8 38.1 %all-gather.17.cloned.1.call-done = bf16[4864,896]{1,0:T(8,128)(2,1)} async-done(((bf16[1216,896]{1,0:T(8,128)(2,1)}), bf16[4864,896]{1,0:T(8,128)(2,1)}) %all-gather.17.cloned.1.call-update) | async-done | bytes 8716304 | tf_op jit(solution)/shard_map/all_gather | solution.py:191
  206.9 14.3 %fusion.25 = f32[6,128,4864]{2,1,0:T(8,128)} fusion(bf16[6,128,896]{2,1,0:T(8,128)(2,1)S(1)} %copy-done.21, bf16[4864,896]{1,0:T(8,128)(2,1)} %all-gather.17.cloned.1.call-done), kind=kOutput, calls=%fused_computation.45 | convolution fusion | flops 6694109184 | bytes 25034752 | tf_op jit(solution)/shard_map/std,fd->stf/dot_general | solution.py:203
  221.2 99.7 %all-gather.15.cloned.1.call-done = bf16[2,896,4864]{1,0,2:T(2,128)(2,1)} async-done(((bf16[2,896,1216]{1,0,2:T(2,128)(2,1)}), bf16[2,896,4864]{1,0,2:T(2,128)(2,1)}) %all-gather.15.cloned.1.call-update) | async-done | bytes 17432592 | tf_op jit(solution)/shard_map/all_gather | solution.py:190
  320.9 34.3 %fusion.85 = (bf16[1,896,4864]{1,0,2:T(2,128)(2,1)}, bf16[1,896,4864]{1,0,2:T(2,128)(2,1)}) fusion(bf16[2,896,4864]{1,0,2:T(2,128)(2,1)} %all-gather.15.cloned.1.call-done), kind=kLoop, calls=%fused_computation.143 | loop fusion | bytes 34865152 | tf_op jit(solution)/shard_map/slice | solution.py:194
  355.3 35.7 %copy.123 = bf16[1,896,4864]{2,1,0:T(8,128)(2,1)} copy(bf16[1,896,4864]{1,0,2:T(2,128)(2,1)} %get-tuple-element.338) | data formatting | bytes 17432576
  391.0 35.8 %copy.122 = bf16[1,896,4864]{2,1,0:T(8,128)(2,1)} copy(bf16[1,896,4864]{1,0,2:T(2,128)(2,1)} %get-tuple-element.337) | data formatting | bytes 17432576
  426.8 13.9 %fusion.29 = f32[6,128,4864]{2,1,0:T(8,128)} fusion(bf16[6,128,896]{2,1,0:T(8,128)(2,1)S(1)} %multiply_convert_fusion.2, bf16[1,896,4864]{2,1,0:T(8,128)(2,1)} %copy.123), kind=kOutput, calls=%fused_computation.49 | convolution fusion | flops 6694109184 | bytes 25034752 | tf_op jit(solution)/shard_map/std,df->stf/dot_general | solution.py:196
  440.7 29.1 %fusion.34 = (bf16[1,6,128,4864]{3,2,1,0:T(8,128)(2,1)}, bf16[1,6,128,4864]{3,2,1,0:T(8,128)(2,1)}, bf16[6,128,4864]{2,1,0:T(8,128)(2,1)}) fusion(f32[6,128,4864]{2,1,0:T(8,128)} %fusion.25, f32[6,128,4864]{2,1,0:T(8,128)} %fusion.29, bf16[6,128,896]{2,1,0:T(8,128)(2,1)} %copy-done.22, bf16[1,896,4864]{2,1,0:T(8,128)(2,1)} %copy.122), kind=kOutput, calls=%fused_computation.54 | convolution fusion | flops 6753878016 | bytes 62390272 | tf_op jit(solution)/shard_map/std,df->stf/dot_general | solution.py:193
  469.8 26.2 %fusion.45 = (bf16[896]{0:T(1024)(128)(2,1)}, f32[6,128]{1,0:T(8,128)S(1)}, f32[6,128,896,1]{2,1,0,3:T(8,128)}) fusion(f32[6,128,896]{2,1,0:T(8,128)S(1)} %copy-done.5, f32[6,128]{1,0:T(8,128)S(1)} %fusion.73, f32[896]{0:T(1024)S(1)} %copy-done.44, bf16[2,896,4864,1]{1,0,2,3:T(2,128)(2,1)} %bitcast.207, bf16[1,6,128,4864]{3,2,1,0:T(8,128)(2,1)} %get-tuple-element.335, ...), kind=kOutput, calls=%fused_computation.77 | convolution fusion | flops 13399816192 | bytes 37891328 | tf_op jit(solution)/shard_map/cstf,cdf->std/dot_general | solution.py:209
  511.2 72.5 %while.27 = (s32[]{:T(128)}, f32[6,2,7,128,64]{3,4,2,1,0:T(8,128)S(1)}, bf16[6,1024,256]{1,2,0:T(8,128)(2,1)}, s32[2]{0:T(128)S(1)}, s32[128]{0:T(128)S(1)}, /*i...) while((s32[]{:T(128)}, ...), condition=%wide.region_13.14_spmd, body=%wide.region_10.13_spmd.sunk | while | flops 3587670528 | bytes 135154640 | solution.py:295
  513.9 67.3 %conditional.5 = ((f32[6,2,7,128,64]{3,4,2,1,0:T(8,128)S(1)}, bf16[6,1024,256]{1,2,0:T(8,128)(2,1)})) conditional(s32[]{:T(128)} %convert_element_type.309, (f32[6,2,7,128,64]{3,4,2,1,0:T(8,128)S(1)}, bf16[6,1024,256]{1,2,0:T(8,128)(2,1)}) %tuple.84, (s32[]{:T(128)}, s32[128]{0:T(128)S(1)}, bf16[6,1024,128]{1,2,0:T(8,128)(2,1)}, ...), branch_computations={%region_11.11_spmd, %region_12.12_spmd} | conditional | flops 3587670528 | bytes 135154368 | solution.py:287
  516.2 9.0 fusion.91
  525.4 15.8 %fusion.11 = bf16[6,2,7,128,512]{3,4,2,1,0:T(8,128)(2,1)} fusion(f32[6,2,512,7,128]{4,2,3,1,0:T(8,128)} %fusion.91, f32[6,2,7,128]{3,2,1,0:T(8,128)S(1)} %copy-done.38, f32[6,2,7,128]{3,2,1,0:T(8,128)S(1)} %copy-done.39, pred[128,512]{0,1:T(8,128)(4,1)S(1)} %broadcast_compare_fusion.1, bf16[6,512,2,64,1]{1,3,4,2,0:T(8,128)(2,1)S(1)} %bitcast.213, ...), kind=kOutput, calls=%fused_computation.18 | convolution fusion | flops 743178240 | bytes 35344384 | tf_op jit(solution)/shard_map/while/body/eval_jaxpr/cond/branch_1_fun/sgjtd,srgd->sgjtr/dot_general | solution.py:261
  541.1 7.6 fusion.92
  548.7 9.4 fusion.13
  559.5 15.1 %dynamic_update_slice.2 = bf16[6,1024,256]{1,2,0:T(8,128)(2,1)} dynamic-update-slice(bf16[6,1024,256]{1,2,0:T(8,128)(2,1)} %get-tuple-element.159, bf16[6,512,256]{1,2,0:T(8,128)(2,1)} %pad_maximum_fusion, s32[]{:T(128)} %constant.38.clone, s32[]{:T(128)S(6)} %select_n.17, s32[]{:T(128)} %constant.38.clone) | dynamic-update-slice | bytes 3145732 | tf_op jit(solution)/shard_map/while/body/eval_jaxpr/cond/branch_1_fun/dynamic_update_slice | solution.py:284
  590.9 138.8 %reduce-scatter.8.cloned.1.call-done = bf16[6,128,256]{2,1,0:T(8,128)(2,1)} async-done(((bf16[6,1024,256]{2,1,0:T(8,128)(2,1)}), bf16[6,128,256]{2,1,0:T(8,128)(2,1)}) %reduce-scatter.8.cloned.1.call-update) | async-done | bytes 393232 | tf_op jit(solution)/shard_map/reduce_scatter | solution.py:298
  751.7 12.7 bitcast_convert_fusion.1
  765.8 22.7 %fusion.18 = bf16[2,896,4864]{1,2,0:T(8,128)(2,1)} fusion(bf16[1,6,128,4864]{3,2,1,0:T(8,128)(2,1)} %get-tuple-element.335, bf16[1,6,128,4864]{3,2,1,0:T(8,128)(2,1)} %get-tuple-element.334, bf16[6,128,896]{2,1,0:T(8,128)(2,1)S(1)} %copy-done.23), kind=kOutput, calls=%fused_computation.33 | convolution fusion | flops 13404405760 | bytes 33751040 | tf_op jit(solution)/shard_map/std,cstf->cdf/dot_general | solution.py:206
  810.6 29.0 %reduce-scatter.16.cloned.1.call-done = bf16[224,896]{1,0:T(8,128)(2,1)} async-done(((bf16[896,896]{1,0:T(8,128)(2,1)}), bf16[224,896]{1,0:T(8,128)(2,1)}) %reduce-scatter.16.cloned.1.call-update) | async-done | bytes 401424 | tf_op jit(solution)/shard_map/reduce_scatter | solution.py:369
  839.7 76.6 %reduce-scatter.20.cloned.1.call-done = bf16[1216,896]{1,0:T(8,128)(2,1)} async-done(((bf16[4864,896]{1,0:T(8,128)(2,1)}), bf16[1216,896]{1,0:T(8,128)(2,1)}) %reduce-scatter.20.cloned.1.call-update) | async-done | bytes 2179088 | tf_op jit(solution)/shard_map/reduce_scatter | solution.py:216
  916.2 131.7 %reduce-scatter.18.cloned.1.call-done = bf16[2,896,1216]{1,2,0:T(8,128)(2,1)} async-done(((bf16[2,896,4864]{1,2,0:T(8,128)(2,1)}), bf16[2,896,1216]{1,2,0:T(8,128)(2,1)}) %reduce-scatter.18.cloned.1.call-update) | async-done | bytes 4358160 | tf_op jit(solution)/shard_map/reduce_scatter | solution.py:213
  1049.7 13.7 add_convert_fusion.1
  1065.7 59.0 %all-reduce.21.cloned.1.call-done = (bf16[224]{0:T(256)(128)(2,1)}, bf16[224]{0:T(256)(128)(2,1)}, bf16[224,128]{1,0:T(8,128)(2,1)}, bf16[32]{0:T(256)(128)(2,1)...) async-done(((bf16[224]{0:T(256)(128)(2,1)}, bf16[224]{0:T(256)(128)(2,1)}, bf16[224,128]{1,0:T(8,128)(2,1)}, bf16[32]{0:T(256)(128)(2,1)}, ...) | async-done | bytes 116176 | tf_op jit(solution)/shard_map/psum | solution.py:389
  1133.4 236.3 %all-reduce.23.cloned.1.call-done = (bf16[224,896]{1,0:T(8,128)(2,1)}, bf16[224,896]{1,0:T(8,128)(2,1)}, bf16[2,896,1216]{1,2,0:T(8,128)(2,1)}, bf16[1216,896]{1,0:T(8,128)(2,1)}) async-done(((bf16[224,896]{1,0:T(8,128)(2,1)}, bf16[224,896]{1,0:T(8,128)(2,1)}, bf16[2,896,1216]{1,2,0:T(8,128)(2,1)}, bf16[1216,896]{1,0:T(8,128)(2,1)}), (bf16[224,896]{1,0:T(8,128)(2,1)}, bf16[224,896]{1,0:T(8,128)(2,1)}, ...) | async-done | bytes 7340048 | tf_op jit(solution)/shard_map/psum | solution.py:390
  (245 shorter events, 166.8 us)
Async XLA Ops:
  7.2 28.0 %copy-start.37 = (bf16[224,128]{1,0:T(8,128)(2,1)S(1)}, bf16[224,128]{1,0:T(8,128)(2,1)}, u32[]{:S(2)}) copy-start(bf16[224,128]{1,0:T(8,128)(2,1)} %param.25) | copy-start | bytes 172036
  7.2 57.6 %all-gather.9.cloned.1.call-start = ((), (), s32[]{:S(2)}) async-start(), calls=%async_computation.8 | async-start | bytes 2007040 | tf_op jit(solution)/shard_map/all_gather | solution.py:126
  7.9 33.1 %copy-start.9 = (bf16[6,128,896]{2,1,0:T(8,128)(2,1)S(1)}, bf16[6,128,896]{2,1,0:T(8,128)(2,1)}, u32[]{:S(2)}) copy-start(bf16[6,128,896]{2,1,0:T(8,128)(2,1)} %param.21) | copy-start | bytes 4128772
  7.9 72.5 %all-gather.11.cloned.1.call-start = ((), (), s32[]{:S(2)}) async-start(), calls=%async_computation.9 | async-start | bytes 1769472 | tf_op jit(solution)/shard_map/all_gather | solution.py:173
  23.5 41.3 %copy-start.40 = (f32[896]{0:T(1024)}, f32[896]{0:T(1024)S(1)}, u32[]{:S(2)}) copy-start(f32[896]{0:T(1024)S(1)} %convert_element_type.193) | copy-start | bytes 10756
  32.4 9.3 copy-start.45
  32.5 32.3 %copy-start.42 = (f32[6,128]{1,0:T(8,128)}, f32[6,128]{1,0:T(8,128)S(1)}, u32[]{:S(2)}) copy-start(f32[6,128]{1,0:T(8,128)S(1)} %fusion.72) | copy-start | bytes 9220
  35.1 90.8 %all-gather.7.cloned.1.call-start = ((), (), s32[]{:S(2)}) async-start(), calls=%async_computation.7 | async-start | bytes 1769472 | tf_op jit(solution)/shard_map/all_gather | solution.py:172
  41.0 32.2 %copy-start.31 = (f32[128,64]{0,1:T(8,128)}, f32[128,64]{0,1:T(8,128)S(1)}, u32[]{:S(2)}) copy-start(f32[128,64]{0,1:T(8,128)S(1)} %get-tuple-element.349) | copy-start | bytes 98308
  41.1 32.2 %copy-start.33 = (f32[128,64]{0,1:T(8,128)}, f32[128,64]{0,1:T(8,128)S(1)}, u32[]{:S(2)}) copy-start(f32[128,64]{0,1:T(8,128)S(1)} %get-tuple-element.350) | copy-start | bytes 98308
  42.6 120.1 %all-gather.13.cloned.1.call-start = ((), (), s32[]{:S(2)}) async-start(), calls=%async_computation.10 | async-start | bytes 2007040 | tf_op jit(solution)/shard_map/all_gather | solution.py:132
  43.2 163.7 %all-gather.17.cloned.1.call-start = ((), (), s32[]{:S(2)}) async-start(), calls=%async_computation.12 | async-start | bytes 10895360 | tf_op jit(solution)/shard_map/all_gather | solution.py:191
  43.8 277.2 %all-gather.15.cloned.1.call-start = ((), (), s32[]{:S(2)}) async-start(), calls=%async_computation.11 | async-start | bytes 21790720 | tf_op jit(solution)/shard_map/all_gather | solution.py:190
  63.9 665.7 %reduce-scatter.8.cloned.1.call-start = ((), (), s32[]{:S(2)}) async-start(), calls=%async_computation.13 | async-start | bytes 3538944 | tf_op jit(solution)/shard_map/reduce_scatter | solution.py:298
  167.0 39.9 %copy-start.21 = (bf16[6,128,896]{2,1,0:T(8,128)(2,1)S(1)}, bf16[6,128,896]{2,1,0:T(8,128)(2,1)}, u32[]{:S(2)}) copy-start(bf16[6,128,896]{2,1,0:T(8,128)(2,1)} %param.33) | copy-start | bytes 4128772
  168.8 258.0 %copy-start.22 = (bf16[6,128,896]{2,1,0:T(8,128)(2,1)}, bf16[6,128,896]{2,1,0:T(8,128)(2,1)S(1)}, u32[]{:S(2)}) copy-start(bf16[6,128,896]{2,1,0:T(8,128)(2,1)S(1)} %multiply_convert_fusion.2) | copy-start | bytes 4128772
  440.7 29.1 %copy-start.5 = (f32[6,128,896]{2,1,0:T(8,128)S(1)}, f32[6,128,896]{2,1,0:T(8,128)}, u32[]{:S(2)}) copy-start(f32[6,128,896]{2,1,0:T(8,128)} %copy-done.4) | copy-start | bytes 8257540
  516.2 9.1 copy-start.18
  588.4 222.0 %reduce-scatter.12.cloned.1.call-start = ((), (), s32[]{:S(2)}) async-start(), calls=%async_computation.15 | async-start | bytes 286720 | tf_op jit(solution)/shard_map/reduce_scatter | solution.py:357
  590.9 141.8 %copy-start.41 = (f32[896]{0:T(1024)S(1)}, f32[896]{0:T(1024)}, u32[]{:S(2)}) copy-start(f32[896]{0:T(1024)} %copy-done.40) | copy-start | bytes 10756
  590.9 141.8 %copy-start.43 = (f32[6,128]{1,0:T(8,128)S(1)}, f32[6,128]{1,0:T(8,128)}, u32[]{:S(2)}) copy-start(f32[6,128]{1,0:T(8,128)} %copy-done.42) | copy-start | bytes 9220
  735.6 74.8 %reduce-scatter.14.cloned.1.call-start = ((), (), s32[]{:S(2)}) async-start(), calls=%async_computation.16 | async-start | bytes 286720 | tf_op jit(solution)/shard_map/reduce_scatter | solution.py:363
  740.9 69.7 %reduce-scatter.10.cloned.1.call-start = ((), (), s32[]{:S(2)}) async-start(), calls=%async_computation.14 | async-start | bytes 2007040 | tf_op jit(solution)/shard_map/reduce_scatter | solution.py:351
  747.5 92.1 %reduce-scatter.16.cloned.1.call-start = ((), (), s32[]{:S(2)}) async-start(), calls=%async_computation.17 | async-start | bytes 2007040 | tf_op jit(solution)/shard_map/reduce_scatter | solution.py:369
  751.7 164.5 %reduce-scatter.20.cloned.1.call-start = ((), (), s32[]{:S(2)}) async-start(), calls=%async_computation.19 | async-start | bytes 10895360 | tf_op jit(solution)/shard_map/reduce_scatter | solution.py:216
  764.5 283.4 %reduce-scatter.18.cloned.1.call-start = ((), (), s32[]{:S(2)}) async-start(), calls=%async_computation.18 | async-start | bytes 21790720 | tf_op jit(solution)/shard_map/reduce_scatter | solution.py:213
  788.5 336.2 %all-reduce.21.cloned.1.call-start = ((), (), s32[]{:S(2)}) async-start(), calls=%async_computation.20 | async-start | bytes 234496 | tf_op jit(solution)/shard_map/psum | solution.py:389
  810.4 559.3 %all-reduce.23.cloned.1.call-start = ((), (), s32[]{:S(2)}) async-start(), calls=%async_computation.21 | async-start | bytes 14680064 | tf_op jit(solution)/shard_map/psum | solution.py:390
  1049.7 13.7 copy-start.46
  1049.7 13.7 copy-start.13
  1049.7 13.7 copy-start.16
  1049.7 13.7 copy-start.17
  (31 other events, 112.4 us)
Sparse Core Ops, SparseCore 0:
  9.6 23.8 all-gather.8
  36.2 44.2 all-gather.10
  83.1 42.7 all-gather.6
  127.3 17.9 all-gather.12
  146.7 60.1 all-gather.16
  208.9 112.0 all-gather.14
  588.5 141.1 reduce-scatter.7
  735.7 19.0 reduce-scatter.11
  757.3 19.9 reduce-scatter.13
  780.2 28.5 reduce-scatter.9
  811.3 28.2 reduce-scatter.15
  842.7 73.4 reduce-scatter.19
  918.8 129.0 reduce-scatter.17
  1053.1 71.5 all-reduce.20
  1129.2 240.4 all-reduce.22
where the time goes:
time: 1400 us; the launch traced here: 1390 us
  waiting for transfers between devices  859 us (61%)
  matrix products  233 us (17%)
  local copies, waits for them, and re-layouts  183 us (13%)
  other arithmetic  58.2 us (4%)
  blocking collectives  28.1 us (2%)
  between operations  17.4 us (1%)
    psum x1, waiting for transfers between devices, shards(): lax.psum(owned_qweight.astype(jnp.bfloat16), 'ctx').astype(jnp.float32)  236 us
    reduce_scatter x1, waiting for transfers between devices, shards(): lax.psum_scatter(grad_kv_all.astype(jnp.bfloat16), 'ctx', scatter_dimensi...  139 us
    reduce_scatter x1, waiting for transfers between devices, shards(): lax.psum_scatter(grad_gate_up.astype(jnp.bfloat16), 'fsdp', scatter_dimen...  132 us
    unnamed x105, local copies, waits for them, and re-layouts  109 us
    all_gather x1, waiting for transfers between devices, shards(): lax.all_gather(gate_up, 'fsdp', axis=2, tiled=True)  99.7 us
    reduce_scatter x1, waiting for transfers between devices, shards(): lax.psum_scatter(grad_down.astype(jnp.bfloat16), 'fsdp', scatter_dimensio...  76.6 us
    psum x1, waiting for transfers between devices, shards(): lax.psum(owned_gain_one.astype(jnp.bfloat16), 'ctx').astype(jnp.float32)  59 us
    all_gather x1, waiting for transfers between devices, shards(): lax.all_gather(key_low, 'ctx', axis=1, tiled=True)  43.7 us
  transfers between devices with their start and end apart: 15, of which 10 were waited for; matrix products, arithmetic and copies ran while one was open for 13% of the time, Pallas kernels for 0%

commit v1 on v0

--- a/solution.py
+++ b/solution.py
@@ -186,37 +186,33 @@
     normed_two, norm_two_pull = jax.vjp(rms_norm, hidden, gain_two.astype(jnp.float32))
     normed_two_low = normed_two.astype(jnp.bfloat16)
     cot_f = cotangent.astype(jnp.float32)
-    gate_up_full, down_full = (
-        lax.all_gather(gate_up, "fsdp", axis=2, tiled=True),
-        lax.all_gather(down_weight, "fsdp", axis=0, tiled=True),
-    )
+    normed_two_all = lax.all_gather(normed_two_low, "fsdp", axis=0, tiled=True)
+    cot_all = lax.all_gather(cotangent, "fsdp", axis=0, tiled=True)
     gate_part = jnp.einsum(
-        "std,df->stf", normed_two_low, gate_up_full[0], preferred_element_type=jnp.float32
+        "std,df->stf", normed_two_all, gate_up[0], preferred_element_type=jnp.float32
     )
     up_part = jnp.einsum(
-        "std,df->stf", normed_two_low, gate_up_full[1], preferred_element_type=jnp.float32
+        "std,df->stf", normed_two_all, gate_up[1], preferred_element_type=jnp.float32
     )
     inner_act, swish_pull = jax.vjp(swish, gate_part, up_part)
     inner_low = inner_act.astype(jnp.bfloat16)
-    ffn_term = jnp.einsum("stf,fd->std", inner_low, down_full, preferred_element_type=jnp.float32)
-    grad_down = jnp.einsum("stf,std->fd", inner_low, cotangent, preferred_element_type=jnp.float32)
-    grad_inner = jnp.einsum("std,fd->stf", cotangent, down_full, preferred_element_type=jnp.float32)
+    ffn_part = jnp.einsum("stf,fd->std", inner_low, down_weight, preferred_element_type=jnp.float32)
+    ffn_term = lax.psum_scatter(
+        ffn_part.astype(jnp.bfloat16), "fsdp", scatter_dimension=0, tiled=True
+    ).astype(jnp.float32)
+    grad_down = jnp.einsum("stf,std->fd", inner_low, cot_all, preferred_element_type=jnp.float32)
+    grad_inner = jnp.einsum("std,fd->stf", cot_all, down_weight, preferred_element_type=jnp.float32)
     grad_gate, grad_up = swish_pull(grad_inner)
     grad_pair = jnp.stack([grad_gate, grad_up]).astype(jnp.bfloat16)
     grad_gate_up = jnp.einsum(
-        "std,cstf->cdf", normed_two_low, grad_pair, preferred_element_type=jnp.float32
-    )
-    grad_normed_two = jnp.einsum(
-        "cstf,cdf->std", grad_pair, gate_up_full, preferred_element_type=jnp.float32
-    )
-    grad_gate_up, grad_down = (
-        lax.psum_scatter(
-            grad_gate_up.astype(jnp.bfloat16), "fsdp", scatter_dimension=2, tiled=True
-        ).astype(jnp.float32),
-        lax.psum_scatter(
-            grad_down.astype(jnp.bfloat16), "fsdp", scatter_dimension=0, tiled=True
-        ).astype(jnp.float32),
-    )
+        "std,cstf->cdf", normed_two_all, grad_pair, preferred_element_type=jnp.float32
+    )
+    grad_normed_two_part = jnp.einsum(
+        "cstf,cdf->std", grad_pair, gate_up, preferred_element_type=jnp.float32
+    )
+    grad_normed_two = lax.psum_scatter(
+        grad_normed_two_part.astype(jnp.bfloat16), "fsdp", scatter_dimension=0, tiled=True
+    ).astype(jnp.float32)
     layer_out = (hidden + ffn_term).astype(jnp.bfloat16)
     grad_hidden_norm, grad_gain_two = norm_two_pull(grad_normed_two)
     grad_hidden = cot_f + grad_hidden_norm

time: 1400 us -> 1130 us (0.81)
  waiting for transfers between devices: 859 us -> 717 us
  local copies, waits for them, and re-layouts: 183 us -> 69.7 us
  matrix products: 233 us -> 216 us
    reduce_scatter x2, waiting for transfers between devices: 208 us -> 91.8 us  [the longest x1 51.8 us: shards(): lax.psum_scatter(ffn_part.astype(jnp.bfloat16), 'fsdp', scatter_dimension...]
    unnamed x105 -> x108, local copies, waits for them, and re-layouts: 109 us -> 22.5 us
    all_gather x2, waiting for transfers between devices: 138 us -> 84.1 us  [the longest x1 65.6 us: shards(): normed_two_all = lax.all_gather(normed_two_low, 'fsdp', axis=0, tiled=True)]
    slice x1 -> x0, local copies, waits for them, and re-layouts: 34.3 us -> none  [shards(): gate_up_full[0]]
    all_gather x1, waiting for transfers between devices: 4.67 us -> 19.8 us  [shards(): lax.all_gather(value_low, 'ctx', axis=1, tiled=True)]
    dot_general x7, matrix products: 133 us -> 117 us  [the longest x1 24.7 us: shards(): jnp.einsum('std,fd->stf', cot_all, down_weight, preferred_element_type=jn...]
  transfers between devices with their start and end apart: 15 -> 15, of which waited for: 10 -> 11; matrix products, arithmetic and copies ran while one was open for 13% -> 17% of each run, Pallas kernels for 0% -> 0%
where the time goes in v1:
time: 1130 us
  waiting for transfers between devices  717 us (63%)
  matrix products  216 us (19%)
  other arithmetic  72.1 us (6%)
  local copies, waits for them, and re-layouts  69.7 us (6%)
  blocking collectives  27.7 us (2%)
  between operations  17.5 us (2%)
    psum x1, waiting for transfers between devices, shards(): lax.psum(owned_qweight.astype(jnp.bfloat16), 'ctx').astype(jnp.float32)  237 us
    reduce_scatter x1, waiting for transfers between devices, shards(): lax.psum_scatter(grad_kv_all.astype(jnp.bfloat16), 'ctx', scatter_dimensi...  137 us
    psum x1, waiting for transfers between devices, shards(): lax.psum(owned_gain_one.astype(jnp.bfloat16), 'ctx').astype(jnp.float32)  71.2 us
    all_gather x1, waiting for transfers between devices, shards(): normed_two_all = lax.all_gather(normed_two_low, 'fsdp', axis=0, tiled=True)  65.6 us
    reduce_scatter x1, waiting for transfers between devices, shards(): lax.psum_scatter(ffn_part.astype(jnp.bfloat16), 'fsdp', scatter_dimension...  51.8 us
    all_gather x1, waiting for transfers between devices, shards(): lax.all_gather(key_low, 'ctx', axis=1, tiled=True)  42.9 us
    reduce_scatter x1, waiting for transfers between devices, shards(): lax.psum_scatter(grad_normed_two_part.astype(jnp.bfloat16), 'fsdp', scatt...  40 us
    reduce_scatter x1, waiting for transfers between devices, shards(): lax.psum_scatter(grad_output.astype(jnp.bfloat16), 'fsdp', scatter_dimens...  30.7 us
  transfers between devices with their start and end apart: 15, of which 11 were waited for; matrix products, arithmetic and copies ran while one was open for 17% of the time, Pallas kernels for 0%

profile of v1, /device:TPU:0, one launch (start us, length us, event | category | flops | bytes accessed | tf_op | source)
XLA Modules:
  0.0 1128.2 jit_solution(17762401295805121877)
XLA Ops:
  20.0 9.9 all-reduce.17
  67.6 19.8 %all-gather.11.cloned.1.call-done = bf16[6,1024,128]{2,1,0:T(8,128)(2,1)} async-done(((bf16[6,128,128]{2,1,0:T(8,128)(2,1)}), bf16[6,1024,128]{2,1,0:T(8,128)(2,1)}) %all-gather.11.cloned.1.call-update) | async-done | bytes 1572880 | tf_op jit(solution)/shard_map/all_gather | solution.py:173
  90.0 42.9 %all-gather.7.cloned.1.call-done = bf16[6,1024,128]{1,2,0:T(8,128)(2,1)} async-done(((bf16[6,128,128]{1,2,0:T(8,128)(2,1)}), bf16[6,1024,128]{1,2,0:T(8,128)(2,1)}) %all-gather.7.cloned.1.call-update) | async-done | bytes 1572880 | tf_op jit(solution)/shard_map/all_gather | solution.py:172
  136.5 34.0 %while.26 = (s32[]{:T(128)}, f32[6,2,7,128]{3,2,1,0:T(8,128)}, f32[6,2,7,128]{3,2,1,0:T(8,128)}, f32[6,2,7,128,64]{3,4,2,1,0:T(8,128)}, s32[2]{0:T(128)}, /*inde...) while((s32[]{:T(128)}, f32[6,2,7,128]{3,2,1,0:T(8,128)}, ...), condition=%wide.region_6.7_spmd, body=%wide.region_1.6_spmd.sunk | while | flops 1482315264 | bytes 167214064 | solution.py:87
  140.3 26.0 %conditional.4 = ((f32[6,2,7,128]{3,2,1,0:T(8,128)}, f32[6,2,7,128]{3,2,1,0:T(8,128)}, f32[6,2,7,128,64]{3,4,2,1,0:T(8,128)})) conditional(s32[]{:T(128)} %convert_element_type.337, (f32[6,2,7,128]{3,2,1,0:T(8,128)}, f32[6,2,7,128]{3,2,1,0:T(8,128)}, f32[6,2,7,128,64]{3,4,2,1,0:T(8,128)}) %tuple.80, (s32[]{:T(128)}, s32[128]{0:T(128)}, s32[]{:T(128)}, ...), branch_computations={%region_2.2_spmd, %region_3.5_spmd} | conditional | flops 1482315264 | bytes 167213792 | solution.py:83
  145.8 6.8 fusion.2
  153.2 12.5 %multiply_add_fusion = f32[6,2,7,128,64]{3,4,2,1,0:T(8,128)} fusion(f32[6,2,7,128,64]{3,4,2,1,0:T(8,128)} %get-tuple-element.135, bf16[6,512,2,64,1]{1,3,4,2,0:T(8,128)(2,1)S(1)} %bitcast.210, f32[6,2,512,7,128]{4,2,3,1,0:T(8,128)} %copy-done.2, f32[6,2,7,128]{3,2,1,0:T(8,128)S(1)} %max.2, pred[128,512]{0,1:T(8,128)(4,1)S(1)} %broadcast_compare_fusion, ...), kind=kOutput, calls=%fused_computation.7 | convolution fusion | flops 733544448 | bytes 28463104 | tf_op jit(solution)/shard_map/while/body/eval_jaxpr/cond/branch_1_fun/sgjtr,srgd->sgjtd/dot_general | solution.py:74
  181.8 65.6 %all-gather.15.cloned.1.call-done = bf16[24,128,896]{2,1,0:T(8,128)(2,1)} async-done(((bf16[6,128,896]{2,1,0:T(8,128)(2,1)}), bf16[24,128,896]{2,1,0:T(8,128)(2,1)}) %all-gather.15.cloned.1.call-update) | async-done | bytes 5505040 | tf_op jit(solution)/shard_map/all_gather | solution.py:189
  247.4 13.1 %fusion.50 = f32[24,128,1216]{1,2,0:T(8,128)} fusion(bf16[24,128,896]{2,1,0:T(8,128)(2,1)} %all-gather.15.cloned.1.call-done, bf16[2,896,1216]{1,2,0:T(8,128)(2,1)} %param.31), kind=kOutput, calls=%fused_computation.86 | convolution fusion | flops 6694109184 | bytes 22626304 | tf_op jit(solution)/shard_map/std,df->stf/dot_general | solution.py:194
  260.5 11.8 %fusion.52 = f32[24,128,1216]{1,2,0:T(8,128)} fusion(bf16[24,128,896]{2,1,0:T(8,128)(2,1)S(1)} %copy-done.50, bf16[2,896,1216]{1,2,0:T(8,128)(2,1)} %param.31), kind=kOutput, calls=%fused_computation.88 | convolution fusion | flops 6694109184 | bytes 22626304 | tf_op jit(solution)/shard_map/std,df->stf/dot_general | solution.py:191
  272.3 18.4 %all-gather.17.cloned.1.call-done = bf16[24,128,896]{2,1,0:T(8,128)(2,1)} async-done(((bf16[6,128,896]{2,1,0:T(8,128)(2,1)}), bf16[24,128,896]{2,1,0:T(8,128)(2,1)}) %all-gather.17.cloned.1.call-update) | async-done | bytes 5505040 | tf_op jit(solution)/shard_map/all_gather | solution.py:190
  290.8 24.7 %fusion.25 = (bf16[1,24,128,1216]{2,3,1,0:T(8,128)(2,1)}, bf16[1,24,128,1216]{2,3,1,0:T(8,128)(2,1)}, bf16[24,128,1216]{1,2,0:T(8,128)(2,1)}) fusion(f32[24,128,1216]{1,2,0:T(8,128)} %fusion.52, f32[24,128,1216]{1,2,0:T(8,128)} %fusion.50, bf16[24,128,896]{2,1,0:T(8,128)(2,1)} %all-gather.17.cloned.1.call-done, bf16[1216,896]{1,0:T(8,128)(2,1)S(1)} %copy-done), kind=kOutput, calls=%fused_computation.45 | convolution fusion | flops 6753878016 | bytes 59981824 | tf_op jit(solution)/shard_map/std,fd->stf/dot_general | solution.py:204
  315.5 21.6 %bitcast_convert_fusion = bf16[24,128,896]{2,1,0:T(8,128)(2,1)} fusion(bf16[2,896,1216]{1,2,0:T(8,128)(2,1)} %param.31, bf16[1,24,128,1216]{2,3,1,0:T(8,128)(2,1)} %get-tuple-element.335, bf16[1,24,128,1216]{2,3,1,0:T(8,128)(2,1)} %get-tuple-element.334), kind=kOutput, calls=%fused_computation.40 | convolution fusion | flops 13398441984 | bytes 24805376 | tf_op jit(solution)/shard_map/cstf,cdf->std/dot_general | solution.py:210
  337.2 12.4 %convolution_convert_fusion = bf16[24,128,896]{2,1,0:T(8,128)(2,1)} fusion(bf16[24,128,1216]{1,2,0:T(8,128)(2,1)} %get-tuple-element.336, bf16[1216,896]{1,0:T(8,128)(2,1)S(1)} %copy-done), kind=kOutput, calls=%fused_computation.65 | convolution fusion | flops 6696861696 | bytes 15155200 | tf_op jit(solution)/shard_map/stf,fd->std/dot_general | solution.py:199
  350.4 40.0 %reduce-scatter.10.cloned.1.call-done = bf16[6,128,896]{2,1,0:T(8,128)(2,1)} async-done(((bf16[24,128,896]{2,1,0:T(8,128)(2,1)}), bf16[6,128,896]{2,1,0:T(8,128)(2,1)}) %reduce-scatter.10.cloned.1.call-update) | async-done | bytes 1376272 | tf_op jit(solution)/shard_map/reduce_scatter | solution.py:213
  394.1 51.8 %reduce-scatter.8.cloned.1.call-done = bf16[6,128,896]{2,1,0:T(8,128)(2,1)} async-done(((bf16[24,128,896]{2,1,0:T(8,128)(2,1)}), bf16[6,128,896]{2,1,0:T(8,128)(2,1)}) %reduce-scatter.8.cloned.1.call-update) | async-done | bytes 1376272 | tf_op jit(solution)/shard_map/reduce_scatter | solution.py:200
  462.4 72.7 %while.27 = (s32[]{:T(128)}, f32[6,2,7,128,64]{3,4,2,1,0:T(8,128)}, bf16[6,1024,256]{1,2,0:T(8,128)(2,1)}, s32[2]{0:T(128)S(1)}, s32[128]{0:T(128)S(1)}, /*index...) while((s32[]{:T(128)}, f32[6,2,7,128,64]{3,4,2,1,0:T(8,128)}, ...), condition=%wide.region_15.16_spmd, body=%wide.region_12.15_spmd.sunk | while | flops 3587670528 | bytes 123800400 | solution.py:291
  465.1 67.6 %conditional.5 = ((f32[6,2,7,128,64]{3,4,2,1,0:T(8,128)}, bf16[6,1024,256]{1,2,0:T(8,128)(2,1)})) conditional(s32[]{:T(128)} %convert_element_type.338, (f32[6,2,7,128,64]{3,4,2,1,0:T(8,128)}, bf16[6,1024,256]{1,2,0:T(8,128)(2,1)}) %tuple.83, (s32[]{:T(128)}, s32[128]{0:T(128)S(1)}, bf16[6,1024,128]{1,2,0:T(8,128)(2,1)}, ...), branch_computations={%region_13.13_spmd, %region_14.14_spmd} | conditional | flops 3587670528 | bytes 123800136 | solution.py:283
  467.3 9.0 fusion.97
  476.5 14.1 %fusion.11 = bf16[6,2,7,128,512]{3,4,2,1,0:T(8,128)(2,1)} fusion(f32[6,2,512,7,128]{4,2,3,1,0:T(8,128)} %fusion.97, f32[6,2,7,128]{3,2,1,0:T(8,128)S(1)} %get-tuple-element.158, f32[6,2,7,128]{3,2,1,0:T(8,128)S(1)} %get-tuple-element.155, pred[128,512]{0,1:T(8,128)(4,1)S(1)} %broadcast_compare_fusion.1, bf16[6,512,2,64,1]{1,3,4,2,0:T(8,128)(2,1)S(1)} %bitcast.211, ...), kind=kOutput, calls=%fused_computation.18 | convolution fusion | flops 743178240 | bytes 35344384 | tf_op jit(solution)/shard_map/while/body/eval_jaxpr/cond/branch_1_fun/sgjtd,srgd->sgjtr/dot_general | solution.py:257
  490.5 7.6 fusion.98
  498.1 9.7 fusion.13
  509.2 15.1 %dynamic_update_slice.2 = bf16[6,1024,256]{1,2,0:T(8,128)(2,1)} dynamic-update-slice(bf16[6,1024,256]{1,2,0:T(8,128)(2,1)} %get-tuple-element.159, bf16[6,512,256]{1,2,0:T(8,128)(2,1)} %pad_maximum_fusion, s32[]{:T(128)} %constant.38.clone, s32[]{:T(128)S(6)} %select_n.17, s32[]{:T(128)} %constant.38.clone) | dynamic-update-slice | bytes 3145732 | tf_op jit(solution)/shard_map/while/body/eval_jaxpr/cond/branch_1_fun/dynamic_update_slice | solution.py:280
  524.3 8.4 convolution_add_fusion
  544.4 136.9 %reduce-scatter.12.cloned.1.call-done = bf16[6,128,256]{2,1,0:T(8,128)(2,1)} async-done(((bf16[6,1024,256]{2,1,0:T(8,128)(2,1)}), bf16[6,128,256]{2,1,0:T(8,128)(2,1)}) %reduce-scatter.12.cloned.1.call-update) | async-done | bytes 393232 | tf_op jit(solution)/shard_map/reduce_scatter | solution.py:294
  702.8 20.9 %fusion.28 = bf16[2,896,1216]{1,2,0:T(8,128)(2,1)} fusion(bf16[24,128,896]{2,1,0:T(8,128)(2,1)} %all-gather.15.cloned.1.call-done, bf16[1,24,128,1216]{2,3,1,0:T(8,128)(2,1)} %get-tuple-element.335, bf16[1,24,128,1216]{2,3,1,0:T(8,128)(2,1)} %get-tuple-element.334), kind=kOutput, calls=%fused_computation.56 | convolution fusion | flops 13397868544 | bytes 24805376 | tf_op jit(solution)/shard_map/std,cstf->cdf/dot_general | solution.py:207
  734.2 6.0 all-reduce.16
  743.5 13.0 %bitcast_convert_fusion.2 = bf16[1216,896]{1,0:T(8,128)(2,1)} fusion(bf16[24,128,1216]{1,2,0:T(8,128)(2,1)} %get-tuple-element.336, bf16[24,128,896]{2,1,0:T(8,128)(2,1)} %all-gather.17.cloned.1.call-done), kind=kOutput, calls=%fused_computation.53 | convolution fusion | flops 6695198720 | bytes 15155200 | tf_op jit(solution)/shard_map/stf,std->fd/dot_general | solution.py:203
  757.2 30.7 %reduce-scatter.20.cloned.1.call-done = bf16[224,896]{1,0:T(8,128)(2,1)} async-done(((bf16[896,896]{1,0:T(8,128)(2,1)}), bf16[224,896]{1,0:T(8,128)(2,1)}) %reduce-scatter.20.cloned.1.call-update) | async-done | bytes 401424 | tf_op jit(solution)/shard_map/reduce_scatter | solution.py:365
  793.5 71.2 %all-reduce.21.cloned.1.call-done = (bf16[224]{0:T(256)(128)(2,1)}, bf16[224]{0:T(256)(128)(2,1)}, bf16[224,128]{1,0:T(8,128)(2,1)}, bf16[32]{0:T(256)(128)(2,1)...) async-done(((bf16[224]{0:T(256)(128)(2,1)}, bf16[224]{0:T(256)(128)(2,1)}, bf16[224,128]{1,0:T(8,128)(2,1)}, bf16[32]{0:T(256)(128)(2,1)}, ...) | async-done | bytes 116176 | tf_op jit(solution)/shard_map/psum | solution.py:385
  873.6 236.8 %all-reduce.23.cloned.1.call-done = (bf16[224,896]{1,0:T(8,128)(2,1)}, bf16[224,896]{1,0:T(8,128)(2,1)}, bf16[2,896,1216]{1,2,0:T(8,128)(2,1)}, bf16[1216,896]{1,0:T(8,128)(2,1)}) async-done(((bf16[224,896]{1,0:T(8,128)(2,1)}, bf16[224,896]{1,0:T(8,128)(2,1)}, bf16[2,896,1216]{1,2,0:T(8,128)(2,1)}, bf16[1216,896]{1,0:T(8,128)(2,1)}), (bf16[224,896]{1,0:T(8,128)(2,1)}, bf16[224,896]{1,0:T(8,128)(2,1)}, ...) | async-done | bytes 7340048 | tf_op jit(solution)/shard_map/psum | solution.py:386
  1110.3 6.4 convert_element_type.247
  (248 shorter events, 166.7 us)
Async XLA Ops:
  7.2 283.6 %copy-start = (bf16[1216,896]{1,0:T(8,128)(2,1)S(1)}, bf16[1216,896]{1,0:T(8,128)(2,1)}, u32[]{:S(2)}) copy-start(bf16[1216,896]{1,0:T(8,128)(2,1)} %param.32) | copy-start | bytes 6537220
  7.2 49.0 %all-gather.9.cloned.1.call-start = ((), (), s32[]{:S(2)}) async-start(), calls=%async_computation.8 | async-start | bytes 2007040 | tf_op jit(solution)/shard_map/all_gather | solution.py:126
  7.9 42.1 %copy-start.5 = (bf16[6,128,896]{2,1,0:T(8,128)(2,1)S(1)}, bf16[6,128,896]{2,1,0:T(8,128)(2,1)}, u32[]{:S(2)}) copy-start(bf16[6,128,896]{2,1,0:T(8,128)(2,1)} %param.21) | copy-start | bytes 4128772
  7.9 79.5 %all-gather.11.cloned.1.call-start = ((), (), s32[]{:S(2)}) async-start(), calls=%async_computation.9 | async-start | bytes 1769472 | tf_op jit(solution)/shard_map/all_gather | solution.py:173
  30.6 8.9 copy-start.40
  42.8 90.1 %all-gather.7.cloned.1.call-start = ((), (), s32[]{:S(2)}) async-start(), calls=%async_computation.7 | async-start | bytes 1769472 | tf_op jit(solution)/shard_map/all_gather | solution.py:172
  52.3 121.6 %all-gather.13.cloned.1.call-start = ((), (), s32[]{:S(2)}) async-start(), calls=%async_computation.10 | async-start | bytes 2007040 | tf_op jit(solution)/shard_map/all_gather | solution.py:132
  52.9 194.5 %all-gather.15.cloned.1.call-start = ((), (), s32[]{:S(2)}) async-start(), calls=%async_computation.11 | async-start | bytes 6881280 | tf_op jit(solution)/shard_map/all_gather | solution.py:189
  145.8 7.4 copy-start.2
  145.8 7.4 copy-start.12
  153.2 12.5 %copy-start.13 = (f32[6,2,7,128]{3,2,1,0:T(8,128)}, f32[6,2,7,128]{3,2,1,0:T(8,128)S(1)}, u32[]{:S(2)}) copy-start(f32[6,2,7,128]{3,2,1,0:T(8,128)S(1)} %get-tuple-element.492) | copy-start | bytes 129028 | tf_op jit(solution)/shard_map/while/body/eval_jaxpr/cond
  181.2 109.6 %all-gather.17.cloned.1.call-start = ((), (), s32[]{:S(2)}) async-start(), calls=%async_computation.13 | async-start | bytes 6881280 | tf_op jit(solution)/shard_map/all_gather | solution.py:190
  181.8 208.6 %reduce-scatter.10.cloned.1.call-start = ((), (), s32[]{:S(2)}) async-start(), calls=%async_computation.14 | async-start | bytes 6881280 | tf_op jit(solution)/shard_map/reduce_scatter | solution.py:213
  247.4 13.1 %copy-start.50 = (bf16[24,128,896]{2,1,0:T(8,128)(2,1)S(1)}, bf16[24,128,896]{2,1,0:T(8,128)(2,1)}, u32[]{:S(2)}) copy-start(bf16[24,128,896]{2,1,0:T(8,128)(2,1)} %all-gather.15.cloned.1.call-done) | copy-start | bytes 16515076
  337.1 108.8 %reduce-scatter.8.cloned.1.call-start = ((), (), s32[]{:S(2)}) async-start(), calls=%async_computation.12 | async-start | bytes 6881280 | tf_op jit(solution)/shard_map/reduce_scatter | solution.py:200
  349.5 40.8 %copy-start.35 = (f32[896]{0:T(1024)S(1)}, f32[896]{0:T(1024)}, u32[]{:S(2)}) copy-start(f32[896]{0:T(1024)} %convert_element_type.213) | copy-start | bytes 10756
  349.5 40.8 %copy-start.37 = (f32[6,128]{1,0:T(8,128)S(1)}, f32[6,128]{1,0:T(8,128)}, u32[]{:S(2)}) copy-start(f32[6,128]{1,0:T(8,128)} %copy-done.36) | copy-start | bytes 9220
  349.5 44.6 %copy-start.47 = (f32[6,128]{1,0:T(8,128)S(1)}, f32[6,128]{1,0:T(8,128)}, u32[]{:S(2)}) copy-start(f32[6,128]{1,0:T(8,128)} %copy-done.46) | copy-start | bytes 9220
  349.6 96.4 %copy-start.11 = (bf16[6,128,896]{2,1,0:T(8,128)(2,1)S(1)}, bf16[6,128,896]{2,1,0:T(8,128)(2,1)}, u32[]{:S(2)}) copy-start(bf16[6,128,896]{2,1,0:T(8,128)(2,1)} %param.33) | copy-start | bytes 4128772
  349.6 331.8 %reduce-scatter.12.cloned.1.call-start = ((), (), s32[]{:S(2)}) async-start(), calls=%async_computation.15 | async-start | bytes 3538944 | tf_op jit(solution)/shard_map/reduce_scatter | solution.py:294
  539.9 203.3 %reduce-scatter.16.cloned.1.call-start = ((), (), s32[]{:S(2)}) async-start(), calls=%async_computation.17 | async-start | bytes 286720 | tf_op jit(solution)/shard_map/reduce_scatter | solution.py:353
  544.4 138.9 %copy-start.27 = (f32[128,64]{0,1:T(8,128)S(1)}, f32[128,64]{0,1:T(8,128)}, u32[]{:S(2)}) copy-start(f32[128,64]{0,1:T(8,128)} %copy-done.25) | copy-start | bytes 98308
  544.4 139.0 %copy-start.6 = (bf16[6,128,896]{2,1,0:T(8,128)(2,1)S(1)}, bf16[6,128,896]{2,1,0:T(8,128)(2,1)}, u32[]{:S(2)}) copy-start(bf16[6,128,896]{2,1,0:T(8,128)(2,1)} %param.21) | copy-start | bytes 4128772
  544.4 139.0 %copy-start.41 = (f32[896]{0:T(1024)S(1)}, f32[896]{0:T(1024)}, u32[]{:S(2)}) copy-start(f32[896]{0:T(1024)} %copy-done.40) | copy-start | bytes 10756
  544.4 139.0 %copy-start.43 = (f32[6,128]{1,0:T(8,128)S(1)}, f32[6,128]{1,0:T(8,128)}, u32[]{:S(2)}) copy-start(f32[6,128]{1,0:T(8,128)} %copy-done.42) | copy-start | bytes 9220
  684.9 58.2 %reduce-scatter.18.cloned.1.call-start = ((), (), s32[]{:S(2)}) async-start(), calls=%async_computation.18 | async-start | bytes 286720 | tf_op jit(solution)/shard_map/reduce_scatter | solution.py:359
  689.8 67.4 %reduce-scatter.14.cloned.1.call-start = ((), (), s32[]{:S(2)}) async-start(), calls=%async_computation.16 | async-start | bytes 2007040 | tf_op jit(solution)/shard_map/reduce_scatter | solution.py:347
  696.8 91.2 %reduce-scatter.20.cloned.1.call-start = ((), (), s32[]{:S(2)}) async-start(), calls=%async_computation.19 | async-start | bytes 2007040 | tf_op jit(solution)/shard_map/reduce_scatter | solution.py:365
  702.7 21.1 %copy-start.19 = (bf16[6,128,14,64]{1,3,2,0:T(8,128)(2,1)S(1)}, bf16[6,128,14,64]{1,3,2,0:T(8,128)(2,1)}, u32[]{:S(2)}) copy-start(bf16[6,128,14,64]{1,3,2,0:T(8,128)(2,1)} %copy-done.18) | copy-start | bytes 4128772
  702.7 162.0 %all-reduce.21.cloned.1.call-start = ((), (), s32[]{:S(2)}) async-start(), calls=%async_computation.20 | async-start | bytes 234496 | tf_op jit(solution)/shard_map/psum | solution.py:385
  743.2 367.2 %all-reduce.23.cloned.1.call-start = ((), (), s32[]{:S(2)}) async-start(), calls=%async_computation.21 | async-start | bytes 14680064 | tf_op jit(solution)/shard_map/psum | solution.py:386
  1110.3 6.5 copy-start.16
  (34 other events, 80.0 us)
Sparse Core Ops, SparseCore 0:
  9.6 22.7 all-gather.8
  42.9 44.4 all-gather.10
  90.1 42.7 all-gather.6
  134.3 17.9 all-gather.12
  181.3 66.0 all-gather.14
  248.9 41.8 all-gather.16
  337.2 53.0 reduce-scatter.9
  392.9 53.0 reduce-scatter.7
  540.0 141.2 reduce-scatter.11
  685.0 19.0 reduce-scatter.15
  706.6 19.9 reduce-scatter.17
  729.0 28.2 reduce-scatter.13
  759.8 28.1 reduce-scatter.19
  793.2 71.4 all-reduce.20
  869.8 240.4 all-reduce.22
